TPU v7x, 512 devices: a whole 4x8x8 slice. The times are simulated.
512 devices in a mesh: ctx: 64 (over z, y), section: 2 (over x_hi), dp: 4 (over x_lo, core).
Axes of the slice: x: 4 (x_hi: 2, x_lo: 2; x = x_hi * 2 + x_lo), y: 8, z: 8, core: 2. Of those that a mesh axis runs over, the one named last changes fastest.
Arguments:
- query_vectors: bfloat16 [4, 8192, 1792], P('dp', 'ctx', 'section'), may hold values from -16 to 16
- key_vectors: bfloat16 [4, 8192, 256], P('dp', 'ctx', 'section'), may hold values from -16 to 16
- value_vectors: bfloat16 [4, 8192, 256], P('dp', 'ctx', 'section'), may hold values from -6 to 6
- grad_output: bfloat16 [4, 8192, 1792], P('dp', 'ctx', 'section'), may hold values from -24 to 24
- output_dots: float32 [4, 14, 8192], P('dp', 'section', 'ctx'), may hold values from -12 to 12
- frame_ids: int32 [4, 8192], P('dp'), may hold values from 0 to 63, never falling along the last dimension, each value on 1 to 256 neighbouring positions
- visual_rows: int32 [4, 64, 32], P('dp', 'ctx'), may hold values from 0 to 127, as said below
- shuffle_source: int32 [4, 128, 64], P('dp', ('ctx', 'section')), may hold values from 0 to 63, each once within a row
- qkv_weight: bfloat16 [2304, 3584], P(None, ('section', 'dp')), may hold values from -0.125 to 0.125
- projector_weight: bfloat16 [3584, 2560], P(('section', 'dp')), may hold values from -0.09375 to 0.09375
Outputs:
- grad_keys: bfloat16 [4, 8192, 256], P('dp', 'ctx', 'section')
- grad_values: bfloat16 [4, 8192, 256], P('dp', 'ctx', 'section')
- patch_grads: bfloat16 [4, 8192, 640], P('dp', ('ctx', 'section'))
Inputs may be any that keep to these rules, and one draw needn't show every extreme that they name: `frame_ids`: frame numbers never fall along a sequence; a frame holds 1 to 256 tokens. `visual_rows`: each block of 128 tokens lists 32 distinct positions in increasing order. `shuffle_source`: each row is a permutation.
All inputs are finite; a program needn't handle non-finite values.
Results may differ from a plain program's by a relative error of at most 0.014.
Values may be sent and summed in bfloat16 or wider, within the bound.
No kernel may reach another device: no remote copies, remote signals or barrier semaphores. Data moves between devices by JAX's collectives and lax.ppermute only.
A program may use at most 128 MiB of HBM per device.

v0:
```python
import math
import jax
import jax.numpy as jnp
from jax import lax
from jax.sharding import PartitionSpec as P

HEAD_DIM = 128
GROUP = 7
MASKED = -1e30


def shards(
    query_vectors,
    key_vectors,
    value_vectors,
    grad_output,
    output_dots,
    frame_ids,
    visual_rows,
    shuffle_source,
    qkv_weight,
    projector_weight,
):
    position = lax.axis_index("ctx")
    local_rows = query_vectors.shape[1]
    scale_factor = 1.0 / math.sqrt(HEAD_DIM)
    query_heads = query_vectors[0].reshape(local_rows, GROUP, HEAD_DIM)
    grad_heads = grad_output[0].reshape(local_rows, GROUP, HEAD_DIM)
    corrections = output_dots[0]
    frame_line = frame_ids[0]
    seq_total = frame_line.shape[0]
    query_first = position * local_rows
    query_pos = query_first + jnp.arange(local_rows, dtype=jnp.int32)
    query_frames = lax.dynamic_slice_in_dim(frame_line, query_first, local_rows)
    own_pair = jnp.concatenate([key_vectors[0], value_vectors[0]], axis=1)
    all_pairs = lax.all_gather(own_pair, "ctx", axis=0, tiled=True)
    key_all = all_pairs[:, :HEAD_DIM]
    value_all = all_pairs[:, HEAD_DIM:]
    key_pos = jnp.arange(seq_total, dtype=jnp.int32)
    allowed = (key_pos[None, :] <= query_pos[:, None]) | (
        frame_line[None, :] == query_frames[:, None]
    )
    scores = (
        jnp.einsum("qhd,kd->hqk", query_heads, key_all, preferred_element_type=jnp.float32)
        * scale_factor
    )
    masked_scores = jnp.where(allowed[None], scores, MASKED)
    running = masked_scores.max(axis=-1)
    summed = jnp.exp(masked_scores - running[:, :, None]).sum(axis=-1)
    log_total = running + jnp.log(summed)
    probability = jnp.exp(jnp.where(allowed[None], scores - log_total[:, :, None], MASKED))
    probs_low = probability.astype(jnp.bfloat16)
    grad_probs = jnp.einsum(
        "qhd,kd->hqk", grad_heads, value_all, preferred_element_type=jnp.float32
    )
    grad_scores = (probability * (grad_probs - corrections[:, :, None])).astype(jnp.bfloat16)
    grad_query = (
        jnp.einsum("hqk,kd->qhd", grad_scores, key_all, preferred_element_type=jnp.float32)
        * scale_factor
    )
    key_part = (
        jnp.einsum("hqk,qhd->kd", grad_scores, query_heads, preferred_element_type=jnp.float32)
        * scale_factor
    )
    value_part = jnp.einsum(
        "hqk,qhd->kd", probs_low, grad_heads, preferred_element_type=jnp.float32
    )
    summed_grads = lax.psum_scatter(
        jnp.concatenate([key_part, value_part], axis=1), "ctx", scatter_dimension=0, tiled=True
    )
    grad_keys_low = summed_grads[:, :HEAD_DIM].astype(jnp.bfloat16)
    grad_values_low = summed_grads[:, HEAD_DIM:].astype(jnp.bfloat16)
    grad_query_low = grad_query.astype(jnp.bfloat16).reshape(local_rows, GROUP * HEAD_DIM)
    visual_picks = visual_rows[0, 0]
    chosen = jnp.concatenate(
        [grad_query_low[visual_picks], grad_keys_low[visual_picks], grad_values_low[visual_picks]],
        axis=1,
    )
    everyone = lax.all_gather(chosen[None], ("section", "dp"), axis=0, tiled=True)
    groups = lax.axis_size("section")
    replicas = lax.axis_size("dp")
    half_rows = visual_picks.shape[0] // 2
    width_in = chosen.shape[1]
    arranged = (
        everyone.reshape(groups, replicas, 2, half_rows, width_in)
        .transpose(2, 1, 3, 0, 4)
        .reshape(2 * replicas * half_rows, groups * width_in)
    )
    visual_grad = jnp.dot(arranged, qkv_weight, preferred_element_type=jnp.float32).astype(
        jnp.bfloat16
    )
    shuffled = lax.psum_scatter(
        jnp.dot(visual_grad, projector_weight, preferred_element_type=jnp.float32).astype(
            jnp.bfloat16
        ),
        ("section", "dp"),
        scatter_dimension=0,
        tiled=True,
    ).astype(jnp.float32)
    slot_rows = shuffled.reshape(half_rows * 4, projector_weight.shape[1] // 4)
    patches = slot_rows[shuffle_source[0, 0]].astype(jnp.bfloat16)
    return (grad_keys_low[None], grad_values_low[None], patches[None])


def solution(mesh):
    placed = (
        P("dp", "ctx", "section"),
        P("dp", "ctx", "section"),
        P("dp", "ctx", "section"),
        P("dp", "ctx", "section"),
        P("dp", "section", "ctx"),
        P("dp", None),
        P("dp", "ctx", None),
        P("dp", ("ctx", "section"), None),
        P(None, ("section", "dp")),
        P(("section", "dp"), None),
    )
    return jax.shard_map(
        shards,
        mesh=mesh,
        in_specs=placed,
        out_specs=(
            P("dp", "ctx", "section"),
            P("dp", "ctx", "section"),
            P("dp", ("ctx", "section"), None),
        ),
        check_vma=False,
    )
```

profile of v0, /device:TPU:8, one launch (start us, length us, event | category | flops | bytes accessed | tf_op | source)
XLA Modules:
  0.0 487.8 jit_solution(14910348359824243187)
XLA Ops:
  7.2 0.0 copy-start
  7.2 0.0 all-gather.3.cloned.1.call-start
  7.2 1.6 pad_maximum_fusion.2
  8.8 0.0 all-gather.3.cloned.1.call-update
  8.8 0.0 reduce-scatter.3.cloned.1.call-start
  8.9 1.8 copy.28
  10.6 1.8 copy.26
  12.4 0.7 copy.50
  13.1 0.7 dynamic-slice_bitcast_fusion
  13.8 4.3 fusion.13
  18.0 85.1 %all-gather.3.cloned.1.call-done = bf16[8192,256]{1,0:T(8,128)(2,1)} async-done(((bf16[128,256]{1,0:T(8,128)(2,1)}), bf16[8192,256]{1,0:T(8,128)(2,1)}) %all-gather.3.cloned.1.call-update) | async-done | bytes 4194320 | tf_op jit(solution)/shard_map/all_gather | solution.py:36
  103.1 13.1 %fusion.4 = (f32[7,128]{1,0:T(8,128)S(1)}, f32[8192,128,7]{1,0,2:T(8,128)}) fusion(pred[128,8192]{0,1:T(8,128)(4,1)S(1)} %fusion.13, bf16[128,7,128]{0,2,1:T(8,128)(2,1)} %bitcast.90, bf16[8192,256]{1,0:T(8,128)(2,1)} %all-gather.3.cloned.1.call-done), kind=kOutput, calls=%fused_computation.12 | convolution fusion | flops 1901067392 | bytes 32738816 | tf_op jit(solution)/shard_map/qhd,kd->hqk/dot_general | solution.py:44
  116.2 0.0 copy-start.3
  116.2 12.7 %exponential_reduce_fusion = f32[7,128]{1,0:T(8,128)S(1)} fusion(f32[8192,128,7]{1,0,2:T(8,128)} %get-tuple-element.14, f32[7,128]{1,0:T(8,128)S(1)} %get-tuple-element.13, pred[128,8192]{0,1:T(8,128)(4,1)S(1)} %fusion.13), kind=kLoop, calls=%fused_computation.11 | loop fusion | flops 29359232 | bytes 30415872 | tf_op jit(solution)/shard_map/reduce_sum | solution.py:49
  129.0 0.0 copy-done.3
  129.0 0.0 copy-start.1
  129.0 13.4 %fusion.9 = f32[8192,128]{0,1:T(8,128)S(1)} fusion(bf16[128,7,128]{0,2,1:T(8,128)(2,1)S(1)} %bitcast.92, f32[8192,128,7]{1,0,2:T(8,128)} %get-tuple-element.14, f32[7,128]{1,0:T(8,128)S(1)} %log_add_fusion, pred[128,8192]{0,1:T(8,128)(4,1)S(1)} %fusion.13), kind=kOutput, calls=%fused_computation.17 | convolution fusion | flops 1908408320 | bytes 34835968 | tf_op jit(solution)/shard_map/hqk,qhd->kd/dot_general | solution.py:65
  142.4 0.0 copy-done.1
  142.4 0.0 copy-start.2
  142.4 19.4 %fusion.1 = bf16[7,128,8192]{1,2,0:T(8,128)(2,1)} fusion(f32[8192,128,7]{1,0,2:T(8,128)} %get-tuple-element.14, bf16[128,7,128]{0,2,1:T(8,128)(2,1)S(1)} %bitcast.93, f32[7,128]{1,0:T(8,128)S(1)} %bitcast.98, f32[7,128]{1,0:T(8,128)S(1)} %log_add_fusion, pred[128,8192]{0,1:T(8,128)(4,1)S(1)} %fusion.13, bf16[8192,256]{1,0:T(8,128)(2,1)S(1)} %copy-done.1), kind=kOutput, calls=%fused_computation.6 | convolution fusion | flops 1923088384 | bytes 47423488 | tf_op jit(solution)/shard_map/qhd,kd->hqk/dot_general | solution.py:53
  161.8 0.0 copy-done.2
  161.8 9.9 %fusion.12 = f32[8192,128]{0,1:T(8,128)S(1)} fusion(bf16[7,128,8192]{1,2,0:T(8,128)(2,1)} %fusion.1, bf16[128,7,128]{0,2,1:T(8,128)(2,1)S(1)} %bitcast.91), kind=kOutput, calls=%fused_computation.18 | convolution fusion | flops 1880096768 | bytes 19103744 | tf_op jit(solution)/shard_map/hqk,qhd->kd/dot_general | solution.py:62
  171.7 0.0 copy-start.4
  171.7 4.1 pad_maximum_fusion
  175.8 0.0 reduce-scatter.3.cloned.1.call-update
  175.9 0.0 reduce-scatter.5.cloned.1.call-start
  175.9 0.0 copy-done.4
  176.0 0.0 copy-start.5
  176.0 8.2 %fusion.17 = bf16[128,7,128]{2,0,1:T(8,128)(2,1)S(1)} fusion(bf16[7,128,8192]{1,2,0:T(8,128)(2,1)} %fusion.1, bf16[8192,256]{1,0:T(8,128)(2,1)} %all-gather.3.cloned.1.call-done), kind=kOutput, calls=%fused_computation.28 | convolution fusion | flops 1879277568 | bytes 17006592 | tf_op jit(solution)/shard_map/hqk,kd->qhd/dot_general | solution.py:58
  184.2 0.2 copy.34
  184.3 0.6 gather_fusion
  185.0 240.0 %reduce-scatter.3.cloned.1.call-done = f32[128,256]{0,1:T(8,128)} async-done(((f32[8192,256]{0,1:T(8,128)}), f32[128,256]{0,1:T(8,128)}) %reduce-scatter.3.cloned.1.call-update) | async-done | bytes 131088 | tf_op jit(solution)/shard_map/reduce_scatter | solution.py:68
  424.9 0.9 convert.5
  425.9 0.1 copy.36
  426.0 0.6 gather_fusion.2
  426.6 0.1 copy.35
  426.7 0.6 gather_fusion.1
  427.3 13.5 %all-gather = bf16[256,1152]{1,0:T(8,128)(2,1)S(1)} all-gather(bf16[32,1152]{1,0:T(8,128)(2,1)S(1)} %pad_maximum_fusion.1), channel_id=2, replica_groups=mesh['ctx'=64,'section'=2,'dp'=4] {'section','dp'}, dimensions={0}, use_global_device_ids=true | all-gather | bytes 663552 | tf_op jit(solution)/shard_map/all_gather | solution.py:79
  440.8 0.6 copy.37
  441.4 0.1 copy.48
  441.5 0.0 copy-done
  441.5 3.7 convolution_convert_fusion
  445.2 0.0 reduce-scatter.5.cloned.1.call-update
  445.3 0.0 copy-done.5
  445.3 0.7 copy.38
  446.0 0.7 copy.39
  446.8 32.2 %reduce-scatter.5.cloned.1.call-done = bf16[16,2560]{1,0:T(8,128)(2,1)} async-done(((bf16[128,2560]{1,0:T(8,128)(2,1)}), bf16[16,2560]{1,0:T(8,128)(2,1)}) %reduce-scatter.5.cloned.1.call-update) | async-done | bytes 81936 | tf_op jit(solution)/shard_map/reduce_scatter | solution.py:92
  479.0 0.9 reshape.155
  480.0 1.3 gather_fusion.3
  (8 shorter events, 0.1 us)
Async XLA Ops:
  7.2 434.3 %copy-start = (bf16[448,2560]{1,0:T(8,128)(2,1)S(1)}, bf16[448,2560]{1,0:T(8,128)(2,1)}, u32[]{:S(2)}) copy-start(bf16[448,2560]{1,0:T(8,128)(2,1)} %param.19) | copy-start | bytes 6881284
  7.2 95.9 %all-gather.3.cloned.1.call-start = ((), (), s32[]{:S(2)}) async-start(), calls=%async_computation.2 | async-start | bytes 4259840 | tf_op jit(solution)/shard_map/all_gather | solution.py:36
  8.8 416.1 %reduce-scatter.3.cloned.1.call-start = ((), (), s32[]{:S(2)}) async-start(), calls=%async_computation.3 | async-start | bytes 8519680 | tf_op jit(solution)/shard_map/reduce_scatter | solution.py:68
  116.2 12.7 %copy-start.3 = (bf16[1,128,896]{1,2,0:T(8,128)(2,1)S(1)}, bf16[1,128,896]{1,2,0:T(8,128)(2,1)}, u32[]{:S(2)}) copy-start(bf16[1,128,896]{1,2,0:T(8,128)(2,1)} %copy.28) | copy-start | bytes 688132
  129.0 13.4 %copy-start.1 = (bf16[8192,256]{1,0:T(8,128)(2,1)S(1)}, bf16[8192,256]{1,0:T(8,128)(2,1)}, u32[]{:S(2)}) copy-start(bf16[8192,256]{1,0:T(8,128)(2,1)} %all-gather.3.cloned.1.call-done) | copy-start | bytes 12582916
  142.4 19.4 %copy-start.2 = (bf16[1,128,896]{1,2,0:T(8,128)(2,1)S(1)}, bf16[1,128,896]{1,2,0:T(8,128)(2,1)}, u32[]{:S(2)}) copy-start(bf16[1,128,896]{1,2,0:T(8,128)(2,1)} %copy.26) | copy-start | bytes 688132
  171.7 4.2 copy-start.4
  175.9 303.1 %reduce-scatter.5.cloned.1.call-start = ((), (), s32[]{:S(2)}) async-start(), calls=%async_computation.4 | async-start | bytes 737280 | tf_op jit(solution)/shard_map/reduce_scatter | solution.py:92
  176.0 269.3 %copy-start.5 = (s32[1,1,64]{2,1,0:T(1,128)S(1)}, s32[1,1,64]{2,1,0:T(1,128)}, u32[]{:S(2)}) copy-start(s32[1,1,64]{2,1,0:T(1,128)} %param.17) | copy-start | bytes 772
Sparse Core Ops, SparseCore 0:
  11.7 91.4 all-gather.2
  176.0 248.9 reduce-scatter.2
  445.4 33.5 reduce-scatter.4
where the time goes:
time: 489 us; the launch traced here: 488 us
  waiting for transfers between devices  357 us (73%)
  matrix products  67.7 us (14%)
  other arithmetic  23.6 us (5%)
  between operations  13.9 us (3%)
  blocking collectives  13.5 us (3%)
  local copies, waits for them, and re-layouts  11.6 us (2%)
    reduce_scatter x1, waiting for transfers between devices, shards(): lax.psum_scatter(jnp.concatenate([key_part, value_part], axis=1), 'ctx',...  240 us
    all_gather x1, waiting for transfers between devices, shards(): all_pairs = lax.all_gather(own_pair, 'ctx', axis=0, tiled=True)  85.1 us
    reduce_scatter x1, waiting for transfers between devices, shards(): lax.psum_scatter(jnp.dot(visual_grad, projector_weight, preferred_element...  32.2 us
    dot_general x1, matrix products, shards(): jnp.einsum('qhd,kd->hqk', grad_heads, value_all, preferred_element_type=j...  19.4 us
    all_gather x1, blocking collectives, shards(): lax.all_gather(chosen[None], ('section', 'dp'), axis=0, tiled=True)  13.5 us
    dot_general x1, matrix products, shards(): jnp.einsum('hqk,qhd->kd', probs_low, grad_heads, preferred_element_type=j...  13.4 us
    dot_general x1, matrix products, shards(): jnp.einsum('qhd,kd->hqk', query_heads, key_all, preferred_element_type=jn...  13.1 us
    reduce_sum x1, other arithmetic, shards(): summed = jnp.exp(masked_scores - running[:, :, None]).sum(axis=-1)  12.7 us
  transfers between devices with their start and end apart: 3, of which 3 were waited for; matrix products, arithmetic and copies ran while one was open for 4% of the time, Pallas kernels for 0%

commit v1 on v0

--- a/solution.py
+++ b/solution.py
@@ -7,6 +7,13 @@
 HEAD_DIM = 128
 GROUP = 7
 MASKED = -1e30
+
+
+def exchange_gather(shard, name, dim):
+    size = lax.axis_size(name)
+    tiles = jnp.stack([shard for _ in range(size)])
+    tiles = lax.all_to_all(tiles, name, split_axis=0, concat_axis=0)
+    return jnp.concatenate(tiles, axis=dim)
 
 
 def shards(
@@ -33,7 +40,7 @@
     query_pos = query_first + jnp.arange(local_rows, dtype=jnp.int32)
     query_frames = lax.dynamic_slice_in_dim(frame_line, query_first, local_rows)
     own_pair = jnp.concatenate([key_vectors[0], value_vectors[0]], axis=1)
-    all_pairs = lax.all_gather(own_pair, "ctx", axis=0, tiled=True)
+    all_pairs = exchange_gather(own_pair, "ctx", 0)
     key_all = all_pairs[:, :HEAD_DIM]
     value_all = all_pairs[:, HEAD_DIM:]
     key_pos = jnp.arange(seq_total, dtype=jnp.int32)

time: 489 us -> 541 us (1.11)
  waiting for transfers between devices: 357 us -> 391 us
  starting transfers between devices: 0.12 us -> 16.9 us
    all_to_all x0 -> x1, waiting for transfers between devices: none -> 107 us  [exchange_gather(): tiles = lax.all_to_all(tiles, name, split_axis=0, concat_axis=0)]
    all_gather x1 -> x0, waiting for transfers between devices: 85.1 us -> none  [shards(): all_pairs = lax.all_gather(own_pair, 'ctx', axis=0, tiled=True)]
    all_to_all x0 -> x1, starting transfers between devices: none -> 16.8 us  [exchange_gather(): tiles = lax.all_to_all(tiles, name, split_axis=0, concat_axis=0)]
    reduce_scatter x1, waiting for transfers between devices: 240 us -> 251 us  [shards(): lax.psum_scatter(jnp.concatenate([key_part, value_part], axis=1), 'ctx',...]
where the time goes in v1:
time: 541 us; the launch traced here: 540 us
  waiting for transfers between devices  391 us (72%)
  matrix products  68 us (13%)
  other arithmetic  23 us (4%)
  starting transfers between devices  16.9 us (3%)
  between operations  14.2 us (3%)
  local copies, waits for them, and re-layouts  14 us (3%)
  blocking collectives  13.4 us (2%)
    reduce_scatter x1, waiting for transfers between devices, shards(): lax.psum_scatter(jnp.concatenate([key_part, value_part], axis=1), 'ctx',...  251 us
    all_to_all x1, waiting for transfers between devices, exchange_gather(): tiles = lax.all_to_all(tiles, name, split_axis=0, concat_axis=0)  107 us
    reduce_scatter x1, waiting for transfers between devices, shards(): lax.psum_scatter(jnp.dot(visual_grad, projector_weight, preferred_element...  32.3 us
    dot_general x1, matrix products, shards(): jnp.einsum('qhd,kd->hqk', grad_heads, value_all, preferred_element_type=j...  19.8 us
    all_to_all x1, starting transfers between devices, exchange_gather(): tiles = lax.all_to_all(tiles, name, split_axis=0, concat_axis=0)  16.8 us
    all_gather x1, blocking collectives, shards(): lax.all_gather(chosen[None], ('section', 'dp'), axis=0, tiled=True)  13.4 us
    dot_general x1, matrix products, shards(): jnp.einsum('hqk,qhd->kd', probs_low, grad_heads, preferred_element_type=j...  13.2 us
    dot_general x1, matrix products, shards(): jnp.einsum('qhd,kd->hqk', query_heads, key_all, preferred_element_type=jn...  13.1 us
  transfers between devices with their start and end apart: 3, of which 3 were waited for; matrix products, arithmetic and copies ran while one was open for 4% of the time, Pallas kernels for 0%

profile of v1, /device:TPU:8, one launch (start us, length us, event | category | flops | bytes accessed | tf_op | source)
XLA Modules:
  0.0 540.1 jit_solution(11632742201189067926)
XLA Ops:
  7.2 0.0 copy-start
  7.2 0.9 pad_maximum_fusion.2
  8.1 2.4 stack.2
  10.6 16.8 %all-to-all-start = ((bf16[64,128,256]{2,1,0:T(8,128)(2,1)}), bf16[64,128,256]{2,1,0:T(8,128)(2,1)}, u32[]{:S(2)}, u32[]{:S(2)}) async-start(bf16[64,128,256]{2,1,0:T(8,128)(2,1)} %stack.2), calls=%async_computation | async-start | bytes 8388608 | tf_op jit(solution)/shard_map/all_to_all | solution.py:15
  27.3 0.0 reduce-scatter.3.cloned.1.call-start
  27.4 1.8 copy.28
  29.2 1.8 copy.26
  30.9 0.7 copy.50
  31.6 0.7 dynamic-slice_bitcast_fusion
  32.3 4.3 fusion.13
  36.6 107.3 %all-to-all-done = bf16[64,128,256]{2,1,0:T(8,128)(2,1)} async-done(((bf16[64,128,256]{2,1,0:T(8,128)(2,1)}), bf16[64,128,256]{2,1,0:T(8,128)(2,1)}, u32[]{:S(2)}, u32[]{:S(2)}) %all-to-all-start) | async-done | bytes 4194336 | tf_op jit(solution)/shard_map/all_to_all | solution.py:15
  143.9 13.1 %fusion.4 = (f32[7,128]{1,0:T(8,128)S(1)}, f32[8192,128,7]{1,0,2:T(8,128)}) fusion(pred[128,8192]{0,1:T(8,128)(4,1)S(1)} %fusion.13, bf16[128,7,128]{0,2,1:T(8,128)(2,1)} %bitcast.91, bf16[8192,256]{1,0:T(8,128)(2,1)} %bitcast.4), kind=kOutput, calls=%fused_computation.12 | convolution fusion | flops 1901067392 | bytes 32738816 | tf_op jit(solution)/shard_map/qhd,kd->hqk/dot_general | solution.py:51
  157.0 0.0 copy-start.2
  157.0 12.7 %exponential_reduce_fusion = f32[7,128]{1,0:T(8,128)S(1)} fusion(f32[8192,128,7]{1,0,2:T(8,128)} %get-tuple-element.14, f32[7,128]{1,0:T(8,128)S(1)} %get-tuple-element.13, pred[128,8192]{0,1:T(8,128)(4,1)S(1)} %fusion.13), kind=kLoop, calls=%fused_computation.11 | loop fusion | flops 29359232 | bytes 30415872 | tf_op jit(solution)/shard_map/reduce_sum | solution.py:56
  169.7 0.0 copy-done.2
  169.7 13.2 %fusion.9 = f32[8192,128]{0,1:T(8,128)S(1)} fusion(bf16[128,7,128]{0,2,1:T(8,128)(2,1)S(1)} %bitcast.93, f32[8192,128,7]{1,0,2:T(8,128)} %get-tuple-element.14, f32[7,128]{1,0:T(8,128)S(1)} %log_add_fusion, pred[128,8192]{0,1:T(8,128)(4,1)S(1)} %fusion.13), kind=kOutput, calls=%fused_computation.17 | convolution fusion | flops 1908408320 | bytes 34835968 | tf_op jit(solution)/shard_map/hqk,qhd->kd/dot_general | solution.py:72
  183.0 0.0 copy-start.1
  183.0 19.8 %fusion.1 = bf16[7,128,8192]{1,2,0:T(8,128)(2,1)} fusion(f32[8192,128,7]{1,0,2:T(8,128)} %get-tuple-element.14, bf16[128,7,128]{0,2,1:T(8,128)(2,1)S(1)} %bitcast.94, f32[7,128]{1,0:T(8,128)S(1)} %bitcast.99, f32[7,128]{1,0:T(8,128)S(1)} %log_add_fusion, pred[128,8192]{0,1:T(8,128)(4,1)S(1)} %fusion.13, bf16[8192,256]{1,0:T(8,128)(2,1)} %bitcast.4), kind=kOutput, calls=%fused_computation.6 | convolution fusion | flops 1923088384 | bytes 47422464 | tf_op jit(solution)/shard_map/qhd,kd->hqk/dot_general | solution.py:60
  202.8 0.0 copy-done.1
  202.8 9.9 %fusion.12 = f32[8192,128]{0,1:T(8,128)S(1)} fusion(bf16[7,128,8192]{1,2,0:T(8,128)(2,1)} %fusion.1, bf16[128,7,128]{0,2,1:T(8,128)(2,1)S(1)} %bitcast.92), kind=kOutput, calls=%fused_computation.18 | convolution fusion | flops 1880096768 | bytes 19103744 | tf_op jit(solution)/shard_map/hqk,qhd->kd/dot_general | solution.py:69
  212.7 0.0 copy-start.3
  212.7 4.1 pad_maximum_fusion
  216.8 0.0 reduce-scatter.3.cloned.1.call-update
  216.9 0.0 reduce-scatter.5.cloned.1.call-start
  216.9 0.0 copy-done.3
  216.9 0.0 copy-start.4
  217.0 8.2 %fusion.17 = bf16[128,7,128]{2,0,1:T(8,128)(2,1)S(1)} fusion(bf16[7,128,8192]{1,2,0:T(8,128)(2,1)} %fusion.1, bf16[8192,256]{1,0:T(8,128)(2,1)} %bitcast.4), kind=kOutput, calls=%fused_computation.28 | convolution fusion | flops 1879277568 | bytes 17006592 | tf_op jit(solution)/shard_map/hqk,kd->qhd/dot_general | solution.py:65
  225.2 0.2 copy.34
  225.3 0.6 gather_fusion
  226.0 250.9 %reduce-scatter.3.cloned.1.call-done = f32[128,256]{0,1:T(8,128)} async-done(((f32[8192,256]{0,1:T(8,128)}), f32[128,256]{0,1:T(8,128)}) %reduce-scatter.3.cloned.1.call-update) | async-done | bytes 131088 | tf_op jit(solution)/shard_map/reduce_scatter | solution.py:75
  476.9 0.9 convert.5
  477.8 0.1 copy.36
  477.9 0.6 gather_fusion.2
  478.5 0.1 copy.35
  478.6 0.6 gather_fusion.1
  479.3 13.4 %all-gather = bf16[256,1152]{1,0:T(8,128)(2,1)S(1)} all-gather(bf16[32,1152]{1,0:T(8,128)(2,1)S(1)} %pad_maximum_fusion.1), channel_id=2, replica_groups=mesh['ctx'=64,'section'=2,'dp'=4] {'section','dp'}, dimensions={0}, use_global_device_ids=true | all-gather | bytes 663552 | tf_op jit(solution)/shard_map/all_gather | solution.py:86
  492.7 0.6 copy.37
  493.3 0.1 copy.48
  493.4 0.0 copy-done
  493.4 3.7 convolution_convert_fusion
  497.1 0.0 reduce-scatter.5.cloned.1.call-update
  497.1 0.0 copy-done.4
  497.2 0.7 copy.38
  497.9 0.7 copy.39
  498.6 32.3 %reduce-scatter.5.cloned.1.call-done = bf16[16,2560]{1,0:T(8,128)(2,1)} async-done(((bf16[128,2560]{1,0:T(8,128)(2,1)}), bf16[16,2560]{1,0:T(8,128)(2,1)}) %reduce-scatter.5.cloned.1.call-update) | async-done | bytes 81936 | tf_op jit(solution)/shard_map/reduce_scatter | solution.py:99
  530.9 0.9 reshape.161
  531.9 1.3 gather_fusion.3
  (8 shorter events, 0.1 us)
Async XLA Ops:
  7.2 486.2 %copy-start = (bf16[448,2560]{1,0:T(8,128)(2,1)S(1)}, bf16[448,2560]{1,0:T(8,128)(2,1)}, u32[]{:S(2)}) copy-start(bf16[448,2560]{1,0:T(8,128)(2,1)} %param.19) | copy-start | bytes 6881284
  10.6 133.3 %all-to-all-start = ((bf16[64,128,256]{2,1,0:T(8,128)(2,1)}), bf16[64,128,256]{2,1,0:T(8,128)(2,1)}, u32[]{:S(2)}, u32[]{:S(2)}) async-start(bf16[64,128,256]{2,1,0:T(8,128)(2,1)} %stack.2), calls=%async_computation | async-start | bytes 8388608 | tf_op jit(solution)/shard_map/all_to_all | solution.py:15
  27.3 449.5 %reduce-scatter.3.cloned.1.call-start = ((), (), s32[]{:S(2)}) async-start(), calls=%async_computation.3 | async-start | bytes 8519680 | tf_op jit(solution)/shard_map/reduce_scatter | solution.py:75
  157.0 12.7 %copy-start.2 = (bf16[1,128,896]{1,2,0:T(8,128)(2,1)S(1)}, bf16[1,128,896]{1,2,0:T(8,128)(2,1)}, u32[]{:S(2)}) copy-start(bf16[1,128,896]{1,2,0:T(8,128)(2,1)} %copy.28) | copy-start | bytes 688132
  183.0 19.8 %copy-start.1 = (bf16[1,128,896]{1,2,0:T(8,128)(2,1)S(1)}, bf16[1,128,896]{1,2,0:T(8,128)(2,1)}, u32[]{:S(2)}) copy-start(bf16[1,128,896]{1,2,0:T(8,128)(2,1)} %copy.26) | copy-start | bytes 688132
  212.7 4.2 copy-start.3
  216.9 314.1 %reduce-scatter.5.cloned.1.call-start = ((), (), s32[]{:S(2)}) async-start(), calls=%async_computation.4 | async-start | bytes 737280 | tf_op jit(solution)/shard_map/reduce_scatter | solution.py:99
  216.9 280.2 %copy-start.4 = (s32[1,1,64]{2,1,0:T(1,128)S(1)}, s32[1,1,64]{2,1,0:T(1,128)}, u32[]{:S(2)}) copy-start(s32[1,1,64]{2,1,0:T(1,128)} %param.17) | copy-start | bytes 772
Sparse Core Ops, SparseCore 0:
  217.0 259.8 reduce-scatter.2
  497.3 33.6 reduce-scatter.4
